TPU v7x, 128 devices: a whole 4x4x4 slice. The times are simulated.
128 devices in a mesh: ctx: 16 (over y, x), grp: 8 (over z, core).
Axes of the slice: x: 4, y: 4, z: 4, core: 2. Of those that a mesh axis runs over, the one named last changes fastest.
Arguments:
- residual: bfloat16 [8, 2048, 2880], P('grp', 'ctx'), may hold values from -3 to 3
- queries: bfloat16 [8, 2048, 2048], P('grp', 'ctx'), may hold values from -8 to 8
- stretch_kv: bfloat16 [8, 2048, 1024], P('grp', 'ctx'), may hold values from -8 to 8
- cache_kv: bfloat16 [8, 4096, 1024], P('grp', 'ctx'), may hold values from -6 to 6
- doc_lengths: int32 [8, 8], P('grp'), may hold values from 1 to 3072, 6144 in all within a row
- sinks: float32 [32], replicated, may hold values from 2 to 6
- out_proj: bfloat16 [2048, 2880], P('ctx'), may hold values from -0.75 to 0.75
- norm_gain: float32 [2880], replicated, may hold values from 0.1 to 1.9
- router: bfloat16 [2880, 64], replicated, may hold values from -0.109375 to 0.109375
- expert_ids: int32 [8, 2048, 4], P('grp', 'ctx'), may hold values from 0 to 63, all different within a row; in each aligned block of 128 rows (0 to 127, 128 to 255, ..., all dimensions but the last counted through in order) at most 10 rows name the same one
- expert_in: bfloat16 [128, 2880, 1536], P(('ctx', 'grp')), may hold values from -0.109375 to 0.109375
- expert_out: bfloat16 [128, 768, 2880], P(('ctx', 'grp')), may hold values from -0.15625 to 0.15625
Outputs:
- resid_mid: bfloat16 [8, 2048, 2880], P('grp', 'ctx')
- layer_out: bfloat16 [8, 2048, 2880], P('grp', 'ctx')
Inputs may be any that keep to these rules, and one draw needn't show every extreme that they name: `expert_ids`: in the rows of one device (aligned blocks of 128 tokens, sequence after sequence), each expert is named by at most 10 rows, and in some blocks one expert by exactly 10; a token's 4 experts differ. `doc_lengths`: A sequence's 8 lengths sum to 6144; the longest is exactly 3072.
All inputs are finite; a program needn't handle non-finite values.
Results may differ from a plain program's by a relative error of at most 0.015.
Values may be sent and summed in bfloat16 or wider, within the bound.
No kernel may reach another device: no remote copies, remote signals or barrier semaphores. Data moves between devices by JAX's collectives and lax.ppermute only.
A program may use at most 128 MiB of HBM per device.

v0:
```python
import math
import jax
import jax.numpy as jnp
from jax import lax
from jax.sharding import PartitionSpec as P

HEADS = 32
KVH = 8
HD = 64


def doc_index(positions, lengths):
    ends = jnp.cumsum(lengths)
    return jnp.sum((positions[:, None] >= ends[None, :]).astype(jnp.int32), axis=1)


def gated_act(pre, half_width):
    gate = pre[:, :half_width]
    upper = pre[:, half_width:]
    return ((upper + 1.0) * gate * jax.nn.sigmoid(1.702 * gate)).astype(jnp.bfloat16)


def body(
    residual,
    queries,
    stretch_kv,
    cache_kv,
    doc_lengths,
    sinks,
    out_proj,
    norm_gain,
    router,
    expert_ids,
    expert_in,
    expert_out,
):
    tokens = residual.shape[1]
    width = residual.shape[2]
    cache_rows = cache_kv.shape[1]
    kv_cols = stretch_kv.shape[2] // 2
    groups = HEADS // KVH
    ctx_count = lax.axis_size("ctx")
    ctx_here = lax.axis_index("ctx")
    stretch_base = cache_rows * ctx_count
    span = cache_rows + tokens
    query_pos = stretch_base + ctx_here * tokens + jnp.arange(tokens, dtype=jnp.int32)
    lengths = doc_lengths[0]
    query_doc = doc_index(query_pos, lengths)
    query_heads = queries[0].reshape(tokens, KVH, groups, HD)
    sink_grid = sinks.reshape(KVH, groups)
    local_kv = jnp.concatenate([cache_kv[0], stretch_kv[0]], axis=0)
    scale = 1.0 / math.sqrt(HD)

    def key_block(carry, keys_values, first):
        count = keys_values.shape[0]
        rows = first + jnp.arange(count, dtype=jnp.int32)
        source = rows // span
        offset = rows % span
        key_pos = jnp.where(
            offset < cache_rows,
            source * cache_rows + offset,
            stretch_base + source * tokens + offset - cache_rows,
        )
        key_doc = doc_index(key_pos, lengths)
        allowed = (key_pos[None, :] <= query_pos[:, None]) & (
            key_doc[None, :] == query_doc[:, None]
        )
        keys = keys_values[:, :kv_cols].reshape(count, KVH, HD)
        values = keys_values[:, kv_cols:].reshape(count, KVH, HD)
        top, total, numer = carry
        scores = (
            jnp.einsum("qkgd,skd->kgqs", query_heads, keys, preferred_element_type=jnp.float32)
            * scale
        )
        masked = jnp.where(allowed[None, None], scores, -jnp.inf)
        new_top = jnp.maximum(top, jnp.max(masked, axis=-1))
        weights = jnp.where(allowed[None, None], jnp.exp(scores - new_top[..., None]), 0.0)
        shrink = jnp.exp(top - new_top)
        total = total * shrink + jnp.sum(weights, axis=-1)
        numer = numer * shrink[..., None] + jnp.einsum(
            "kgqs,skd->kgqd",
            weights.astype(jnp.bfloat16),
            values,
            preferred_element_type=jnp.float32,
        )
        return (new_top, total, numer)

    start_top = jnp.broadcast_to(sink_grid[:, :, None], (KVH, groups, tokens))
    start_total = jnp.zeros((KVH, groups, tokens), jnp.float32)
    start_numer = jnp.zeros((KVH, groups, tokens, HD), jnp.float32)
    piece = lax.all_gather(local_kv, "ctx", axis=0, tiled=True)
    count = piece.shape[0]
    step_rows = math.gcd(count, 1024)

    def advance(index, state):
        first = index * step_rows
        part = lax.dynamic_slice_in_dim(piece, first, step_rows, 0)
        return key_block(state, part, first)

    top, total, numer = lax.fori_loop(
        0, count // step_rows, advance, (start_top, start_total, start_numer)
    )
    denom = total + jnp.exp(sink_grid[:, :, None] - top)
    attended = (
        jnp.transpose(numer / denom[..., None], (2, 0, 1, 3))
        .reshape(tokens, HEADS * HD)
        .astype(jnp.bfloat16)
    )
    grp_here = lax.axis_index("grp")
    parity = grp_here % 2
    grp_count = lax.axis_size("grp")
    pair_perm = [(g, g ^ 1) for g in range(grp_count)]
    head_rows = out_proj.shape[0] // 2
    proj_half = lax.all_gather(
        lax.dynamic_slice_in_dim(out_proj, parity * head_rows, head_rows, 0),
        "ctx",
        axis=0,
        tiled=True,
    )
    by_parity = attended.reshape(tokens, HEADS // 2, 2, HD)
    mine = jnp.where(parity == 0, by_parity[:, :, 0], by_parity[:, :, 1]).reshape(tokens, -1)
    theirs_cols = jnp.where(parity == 0, by_parity[:, :, 1], by_parity[:, :, 0]).reshape(tokens, -1)
    partner_cols = lax.ppermute(theirs_cols, "grp", pair_perm)
    both = jnp.dot(
        jnp.concatenate([mine, partner_cols], axis=0), proj_half, preferred_element_type=jnp.float32
    )
    back = lax.ppermute(both[tokens:], "grp", pair_perm)
    projected = both[:tokens] + back
    mid = (residual[0].astype(jnp.float32) + projected).astype(jnp.bfloat16)
    mid_float = mid.astype(jnp.float32)
    normed = (
        mid_float
        * lax.rsqrt(jnp.mean(mid_float * mid_float, axis=-1, keepdims=True) + 1e-05)
        * norm_gain
    ).astype(jnp.bfloat16)
    logits = jnp.dot(normed, router, preferred_element_type=jnp.float32)
    experts = router.shape[1]
    chosen_ids = expert_ids[0]
    topk = chosen_ids.shape[1]
    picks = chosen_ids[:, :, None] == jnp.arange(experts, dtype=jnp.int32)[None, None, :]
    chosen = jnp.sum(jnp.where(picks, logits[:, None, :], 0.0), axis=-1)
    raised = jnp.exp(chosen)
    route_weights = raised / jnp.sum(raised, axis=-1, keepdims=True)
    capacity = 2 * ((5 * tokens * topk + 8 * experts - 1) // (8 * experts))
    flat_ids = chosen_ids.reshape(-1)
    pairs = flat_ids.shape[0]
    onehot = (flat_ids[:, None] == jnp.arange(experts, dtype=jnp.int32)[None, :]).astype(jnp.int32)
    slots = jnp.sum(onehot * (jnp.cumsum(onehot, axis=0) - 1), axis=1)
    dest = flat_ids * capacity + slots
    source_rows = jnp.arange(pairs, dtype=jnp.int32) // topk
    packed = jnp.zeros((experts * capacity, width), jnp.bfloat16).at[dest].set(normed[source_rows])
    packed = packed.reshape(experts, capacity, width)
    in_weights = expert_in[0]
    out_weights = expert_out[0]
    half_width = out_weights.shape[0]
    owners = 2 * experts
    half_cap = capacity // 2
    split = packed.reshape(owners, half_cap, width)
    received = lax.all_to_all(split, ("ctx", "grp"), split_axis=0, concat_axis=0, tiled=True)
    partner_rows = lax.ppermute(received, "grp", pair_perm)

    def expert_half(rows):
        pre = jnp.dot(rows.reshape(-1, width), in_weights, preferred_element_type=jnp.float32)
        hidden = gated_act(pre, half_width)
        return jnp.dot(hidden, out_weights, preferred_element_type=jnp.float32).astype(jnp.bfloat16)

    own_part = expert_half(received)
    partner_part = expert_half(partner_rows)
    partner_back = lax.ppermute(partner_part, "grp", pair_perm)
    summed = (own_part.astype(jnp.float32) + partner_back.astype(jnp.float32)).astype(jnp.bfloat16)
    returned = lax.all_to_all(
        summed.reshape(owners, half_cap, width),
        ("ctx", "grp"),
        split_axis=0,
        concat_axis=0,
        tiled=True,
    )
    expert_rows = returned.reshape(experts * capacity, width)
    gathered = expert_rows[dest].astype(jnp.float32) * route_weights.reshape(-1)[:, None]
    mixture = jnp.sum(gathered.reshape(tokens, topk, width), axis=1)
    final = (mid_float + mixture).astype(jnp.bfloat16)
    return (mid[None], final[None])


def solution(mesh):
    return jax.shard_map(
        body,
        mesh=mesh,
        in_specs=(
            P("grp", "ctx", None),
            P("grp", "ctx", None),
            P("grp", "ctx", None),
            P("grp", "ctx", None),
            P("grp", None),
            P(),
            P("ctx", None),
            P(),
            P(),
            P("grp", "ctx", None),
            P(("ctx", "grp"), None, None),
            P(("ctx", "grp"), None, None),
        ),
        out_specs=(P("grp", "ctx", None), P("grp", "ctx", None)),
        check_vma=False,
    )
```

profile of v0, /device:TPU:1, one launch (start us, length us, event | category | flops | bytes accessed | tf_op | source)
XLA Modules:
  0.0 601.9 jit_solution(10687653311530739906)
XLA Ops:
  12.9 99.8 %all-gather.3.cloned.1.call-done = bf16[6144,1024]{0,1:T(8,128)(2,1)} async-done(((bf16[384,1024]{0,1:T(8,128)(2,1)}), bf16[6144,1024]{0,1:T(8,128)(2,1)}) %all-gather.3.cloned.1.call-update) | async-done | bytes 12582928 | tf_op jit(solution)/shard_map/all_gather | solution.py:91
  112.8 156.1 %while.20 = (s32[]{:T(128)}, f32[8,4,128]{2,1,0:T(4,128)S(1)}, f32[8,4,128]{2,1,0:T(4,128)S(1)}, f32[8,4,128,64]{2,3,1,0:T(8,128)S(1)}, s32[1,8]{1,0:T(1,128)S(1...) while((s32[]{:T(128)}, f32[8,4,128]{2,1,0:T(4,128)S(1)}, ...), condition=%wide.region_7.8_spmd.clone, body=%wide.region_3.7_spmd.clone.sunk | while | flops 1121116288 | bytes 60053240 | solution.py:100
  115.0 7.1 %fusion.89 = (f32[8,4,128]{2,1,0:T(4,128)S(1)}, f32[8,1024,128,4]{2,1,3,0:T(8,128)}) fusion(pred[128,1024]{0,1:T(8,128)(4,1)S(1)} %compare_and_fusion.2, bf16[1024,8,64,1]{0,2,3,1:T(8,128)(2,1)S(1)} %bitcast.101, bf16[128,8,4,64]{0,3,2,1:T(8,128)(2,1)S(1)} %get-tuple-element.396), kind=kOutput, calls=%fused_computation.6.clone.1 | convolution fusion | flops 549449728 | bytes 18497536 | tf_op jit(solution)/shard_map/while/body/eval_jaxpr/qkgd,skd->kgqs/dot_general | solution.py:72
  122.0 9.5 %fusion.90 = f32[8,4,128]{2,1,0:T(4,128)S(1)} fusion(f32[8,1024,128,4]{2,1,3,0:T(8,128)} %get-tuple-element.357, f32[8,4,128]{2,1,0:T(4,128)S(1)} %max.12, pred[128,1024]{0,1:T(8,128)(4,1)S(1)} %compare_and_fusion.2), kind=kLoop, calls=%fused_computation.10.clone.1 | loop fusion | flops 16773120 | bytes 16941056 | tf_op jit(solution)/shard_map/while/body/eval_jaxpr/reduce_sum | solution.py:79
  131.6 7.6 %fusion.92 = f32[8,4,128,64]{2,3,1,0:T(8,128)S(1)} fusion(bf16[1024,8,64,1]{0,2,3,1:T(8,128)(2,1)S(1)} %bitcast.103, f32[8,1024,128,4]{2,1,3,0:T(8,128)} %get-tuple-element.357, f32[8,4,128]{2,1,0:T(4,128)S(1)} %max.12, pred[128,1024]{0,1:T(8,128)(4,1)S(1)} %compare_and_fusion.2, f32[8,4,128,64]{2,3,1,0:T(8,128)S(1)} %get-tuple-element.378, ...), kind=kOutput, calls=%fused_computation.13.clone.1 | convolution fusion | flops 554434560 | bytes 20086784 | tf_op jit(solution)/shard_map/while/body/eval_jaxpr/kgqs,skd->kgqd/dot_general | solution.py:80
  139.2 1.7 fusion.88
  141.4 7.3 %fusion.89 = (f32[8,4,128]{2,1,0:T(4,128)S(1)}, f32[8,1024,128,4]{2,1,3,0:T(8,128)}) fusion(pred[128,1024]{0,1:T(8,128)(4,1)S(1)} %compare_and_fusion.2, bf16[1024,8,64,1]{0,2,3,1:T(8,128)(2,1)S(1)} %bitcast.101, bf16[128,8,4,64]{0,3,2,1:T(8,128)(2,1)S(1)} %get-tuple-element.396), kind=kOutput, calls=%fused_computation.6.clone.1 | convolution fusion | flops 549449728 | bytes 18497536 | tf_op jit(solution)/shard_map/while/body/eval_jaxpr/qkgd,skd->kgqs/dot_general | solution.py:72
  148.7 9.1 %fusion.90 = f32[8,4,128]{2,1,0:T(4,128)S(1)} fusion(f32[8,1024,128,4]{2,1,3,0:T(8,128)} %get-tuple-element.357, f32[8,4,128]{2,1,0:T(4,128)S(1)} %max.12, pred[128,1024]{0,1:T(8,128)(4,1)S(1)} %compare_and_fusion.2), kind=kLoop, calls=%fused_computation.10.clone.1 | loop fusion | flops 16773120 | bytes 16941056 | tf_op jit(solution)/shard_map/while/body/eval_jaxpr/reduce_sum | solution.py:79
  157.8 7.7 %fusion.92 = f32[8,4,128,64]{2,3,1,0:T(8,128)S(1)} fusion(bf16[1024,8,64,1]{0,2,3,1:T(8,128)(2,1)S(1)} %bitcast.103, f32[8,1024,128,4]{2,1,3,0:T(8,128)} %get-tuple-element.357, f32[8,4,128]{2,1,0:T(4,128)S(1)} %max.12, pred[128,1024]{0,1:T(8,128)(4,1)S(1)} %compare_and_fusion.2, f32[8,4,128,64]{2,3,1,0:T(8,128)S(1)} %get-tuple-element.378, ...), kind=kOutput, calls=%fused_computation.13.clone.1 | convolution fusion | flops 554434560 | bytes 20086784 | tf_op jit(solution)/shard_map/while/body/eval_jaxpr/kgqs,skd->kgqd/dot_general | solution.py:80
  165.6 1.8 fusion.88
  167.9 7.0 %fusion.89 = (f32[8,4,128]{2,1,0:T(4,128)S(1)}, f32[8,1024,128,4]{2,1,3,0:T(8,128)}) fusion(pred[128,1024]{0,1:T(8,128)(4,1)S(1)} %compare_and_fusion.2, bf16[1024,8,64,1]{0,2,3,1:T(8,128)(2,1)S(1)} %bitcast.101, bf16[128,8,4,64]{0,3,2,1:T(8,128)(2,1)S(1)} %get-tuple-element.396), kind=kOutput, calls=%fused_computation.6.clone.1 | convolution fusion | flops 549449728 | bytes 18497536 | tf_op jit(solution)/shard_map/while/body/eval_jaxpr/qkgd,skd->kgqs/dot_general | solution.py:72
  174.9 9.1 %fusion.90 = f32[8,4,128]{2,1,0:T(4,128)S(1)} fusion(f32[8,1024,128,4]{2,1,3,0:T(8,128)} %get-tuple-element.357, f32[8,4,128]{2,1,0:T(4,128)S(1)} %max.12, pred[128,1024]{0,1:T(8,128)(4,1)S(1)} %compare_and_fusion.2), kind=kLoop, calls=%fused_computation.10.clone.1 | loop fusion | flops 16773120 | bytes 16941056 | tf_op jit(solution)/shard_map/while/body/eval_jaxpr/reduce_sum | solution.py:79
  184.0 7.4 %fusion.92 = f32[8,4,128,64]{2,3,1,0:T(8,128)S(1)} fusion(bf16[1024,8,64,1]{0,2,3,1:T(8,128)(2,1)S(1)} %bitcast.103, f32[8,1024,128,4]{2,1,3,0:T(8,128)} %get-tuple-element.357, f32[8,4,128]{2,1,0:T(4,128)S(1)} %max.12, pred[128,1024]{0,1:T(8,128)(4,1)S(1)} %compare_and_fusion.2, f32[8,4,128,64]{2,3,1,0:T(8,128)S(1)} %get-tuple-element.378, ...), kind=kOutput, calls=%fused_computation.13.clone.1 | convolution fusion | flops 554434560 | bytes 20086784 | tf_op jit(solution)/shard_map/while/body/eval_jaxpr/kgqs,skd->kgqd/dot_general | solution.py:80
  191.5 1.7 fusion.88
  193.7 7.0 %fusion.89 = (f32[8,4,128]{2,1,0:T(4,128)S(1)}, f32[8,1024,128,4]{2,1,3,0:T(8,128)}) fusion(pred[128,1024]{0,1:T(8,128)(4,1)S(1)} %compare_and_fusion.2, bf16[1024,8,64,1]{0,2,3,1:T(8,128)(2,1)S(1)} %bitcast.101, bf16[128,8,4,64]{0,3,2,1:T(8,128)(2,1)S(1)} %get-tuple-element.396), kind=kOutput, calls=%fused_computation.6.clone.1 | convolution fusion | flops 549449728 | bytes 18497536 | tf_op jit(solution)/shard_map/while/body/eval_jaxpr/qkgd,skd->kgqs/dot_general | solution.py:72
  200.7 9.1 %fusion.90 = f32[8,4,128]{2,1,0:T(4,128)S(1)} fusion(f32[8,1024,128,4]{2,1,3,0:T(8,128)} %get-tuple-element.357, f32[8,4,128]{2,1,0:T(4,128)S(1)} %max.12, pred[128,1024]{0,1:T(8,128)(4,1)S(1)} %compare_and_fusion.2), kind=kLoop, calls=%fused_computation.10.clone.1 | loop fusion | flops 16773120 | bytes 16941056 | tf_op jit(solution)/shard_map/while/body/eval_jaxpr/reduce_sum | solution.py:79
  209.8 7.4 %fusion.92 = f32[8,4,128,64]{2,3,1,0:T(8,128)S(1)} fusion(bf16[1024,8,64,1]{0,2,3,1:T(8,128)(2,1)S(1)} %bitcast.103, f32[8,1024,128,4]{2,1,3,0:T(8,128)} %get-tuple-element.357, f32[8,4,128]{2,1,0:T(4,128)S(1)} %max.12, pred[128,1024]{0,1:T(8,128)(4,1)S(1)} %compare_and_fusion.2, f32[8,4,128,64]{2,3,1,0:T(8,128)S(1)} %get-tuple-element.378, ...), kind=kOutput, calls=%fused_computation.13.clone.1 | convolution fusion | flops 554434560 | bytes 20086784 | tf_op jit(solution)/shard_map/while/body/eval_jaxpr/kgqs,skd->kgqd/dot_general | solution.py:80
  217.3 1.7 fusion.88
  219.5 7.0 %fusion.89 = (f32[8,4,128]{2,1,0:T(4,128)S(1)}, f32[8,1024,128,4]{2,1,3,0:T(8,128)}) fusion(pred[128,1024]{0,1:T(8,128)(4,1)S(1)} %compare_and_fusion.2, bf16[1024,8,64,1]{0,2,3,1:T(8,128)(2,1)S(1)} %bitcast.101, bf16[128,8,4,64]{0,3,2,1:T(8,128)(2,1)S(1)} %get-tuple-element.396), kind=kOutput, calls=%fused_computation.6.clone.1 | convolution fusion | flops 549449728 | bytes 18497536 | tf_op jit(solution)/shard_map/while/body/eval_jaxpr/qkgd,skd->kgqs/dot_general | solution.py:72
  226.5 9.1 %fusion.90 = f32[8,4,128]{2,1,0:T(4,128)S(1)} fusion(f32[8,1024,128,4]{2,1,3,0:T(8,128)} %get-tuple-element.357, f32[8,4,128]{2,1,0:T(4,128)S(1)} %max.12, pred[128,1024]{0,1:T(8,128)(4,1)S(1)} %compare_and_fusion.2), kind=kLoop, calls=%fused_computation.10.clone.1 | loop fusion | flops 16773120 | bytes 16941056 | tf_op jit(solution)/shard_map/while/body/eval_jaxpr/reduce_sum | solution.py:79
  235.7 7.4 %fusion.92 = f32[8,4,128,64]{2,3,1,0:T(8,128)S(1)} fusion(bf16[1024,8,64,1]{0,2,3,1:T(8,128)(2,1)S(1)} %bitcast.103, f32[8,1024,128,4]{2,1,3,0:T(8,128)} %get-tuple-element.357, f32[8,4,128]{2,1,0:T(4,128)S(1)} %max.12, pred[128,1024]{0,1:T(8,128)(4,1)S(1)} %compare_and_fusion.2, f32[8,4,128,64]{2,3,1,0:T(8,128)S(1)} %get-tuple-element.378, ...), kind=kOutput, calls=%fused_computation.13.clone.1 | convolution fusion | flops 554434560 | bytes 20086784 | tf_op jit(solution)/shard_map/while/body/eval_jaxpr/kgqs,skd->kgqd/dot_general | solution.py:80
  243.1 1.7 fusion.88
  245.3 7.0 %fusion.89 = (f32[8,4,128]{2,1,0:T(4,128)S(1)}, f32[8,1024,128,4]{2,1,3,0:T(8,128)}) fusion(pred[128,1024]{0,1:T(8,128)(4,1)S(1)} %compare_and_fusion.2, bf16[1024,8,64,1]{0,2,3,1:T(8,128)(2,1)S(1)} %bitcast.101, bf16[128,8,4,64]{0,3,2,1:T(8,128)(2,1)S(1)} %get-tuple-element.396), kind=kOutput, calls=%fused_computation.6.clone.1 | convolution fusion | flops 549449728 | bytes 18497536 | tf_op jit(solution)/shard_map/while/body/eval_jaxpr/qkgd,skd->kgqs/dot_general | solution.py:72
  252.3 9.1 %fusion.90 = f32[8,4,128]{2,1,0:T(4,128)S(1)} fusion(f32[8,1024,128,4]{2,1,3,0:T(8,128)} %get-tuple-element.357, f32[8,4,128]{2,1,0:T(4,128)S(1)} %max.12, pred[128,1024]{0,1:T(8,128)(4,1)S(1)} %compare_and_fusion.2), kind=kLoop, calls=%fused_computation.10.clone.1 | loop fusion | flops 16773120 | bytes 16941056 | tf_op jit(solution)/shard_map/while/body/eval_jaxpr/reduce_sum | solution.py:79
  261.5 7.4 %fusion.92 = f32[8,4,128,64]{2,3,1,0:T(8,128)S(1)} fusion(bf16[1024,8,64,1]{0,2,3,1:T(8,128)(2,1)S(1)} %bitcast.103, f32[8,1024,128,4]{2,1,3,0:T(8,128)} %get-tuple-element.357, f32[8,4,128]{2,1,0:T(4,128)S(1)} %max.12, pred[128,1024]{0,1:T(8,128)(4,1)S(1)} %compare_and_fusion.2, f32[8,4,128,64]{2,3,1,0:T(8,128)S(1)} %get-tuple-element.378, ...), kind=kOutput, calls=%fused_computation.13.clone.1 | convolution fusion | flops 554434560 | bytes 20086784 | tf_op jit(solution)/shard_map/while/body/eval_jaxpr/kgqs,skd->kgqd/dot_general | solution.py:80
  271.9 5.3 fusion.52
  283.6 2.0 fusion.39
  286.4 16.3 %scatter_custom_fusion = bf16[640,2880]{1,0:T(8,128)(2,1)} fusion(s32[512]{0:T(512)S(1)} %bitcast.113, bf16[128,2880]{1,0:T(8,128)(2,1)S(1)} %copy.59, s32[1024]{0:T(1024)S(1)} %pad_clamp_fusion.1, bf16[]{:T(256)} %constant.192.clone.1), kind=kCustom, calls=%fused_computation.45 | custom fusion | bytes 3686402 | tf_op jit(solution)/shard_map/scatter | solution.py:151
  302.7 7.4 %reshape_reshape.3 = bf16[128,5,2880]{2,1,0:T(8,128)(2,1)} reshape(bf16[640,2880]{1,0:T(8,128)(2,1)} %scatter_custom_fusion) | data formatting | bytes 7372800 | tf_op jit(solution)/shard_map/reshape;reshape | solution.py:158
  310.1 80.1 %all_to_all.10 = bf16[128,5,2880]{2,1,0:T(8,128)(2,1)} all-to-all(bf16[128,5,2880]{2,1,0:T(8,128)(2,1)} %reshape_reshape.3), channel_id=1, replica_groups=mesh['ctx'=16,'grp'=8] {'ctx','grp'}, dimensions={0} | all-to-all | bytes 7372800 | tf_op jit(solution)/shard_map/all_to_all | solution.py:159
  390.2 7.9 %copy.60 = bf16[128,5,2880]{0,2,1:T(8,128)(2,1)} copy(bf16[128,5,2880]{2,1,0:T(8,128)(2,1)} %all_to_all.10) | data formatting | bytes 7372800 | tf_op jit(solution)/shard_map/all_to_all | solution.py:159
  399.3 6.4 %collective-permute-done.2 = bf16[128,5,2880]{0,2,1:T(8,128)(2,1)} collective-permute-done((bf16[128,5,2880]{0,2,1:T(8,128)(2,1)}, bf16[128,5,2880]{0,2,1:T(8,128)(2,1)}, u32[]{:S(2)}, u32[]{:S(2)}) %collective-permute-start.2) | collective-permute-done | bytes 3686432 | tf_op jit(solution)/shard_map/ppermute | solution.py:160
  405.7 8.5 %copy.61 = bf16[128,5,2880]{2,1,0:T(8,128)(2,1)} copy(bf16[128,5,2880]{0,2,1:T(8,128)(2,1)} %collective-permute-done.2) | data formatting | bytes 7372800 | tf_op jit(solution)/shard_map/ppermute | solution.py:160
  414.2 8.0 %reshape.328 = bf16[640,2880]{1,0:T(8,128)(2,1)} reshape(bf16[128,5,2880]{2,1,0:T(8,128)(2,1)} %copy.61) | data formatting | bytes 7372800 | tf_op jit(solution)/shard_map/reshape | solution.py:163
  422.3 9.9 %fusion.22 = f32[640,1536]{1,0:T(8,128)S(1)} fusion(bf16[640,2880]{1,0:T(8,128)(2,1)} %reshape.328, bf16[1,2880,1536]{2,1,0:T(8,128)(2,1)} %param.24), kind=kOutput, calls=%fused_computation.35 | convolution fusion | flops 5662310400 | bytes 16465920 | tf_op jit(solution)/shard_map/dot_general | solution.py:163
  432.1 7.9 %convolution_convert_fusion = bf16[640,2880]{0,1:T(8,128)(2,1)} fusion(bf16[1,768,2880]{1,2,0:T(8,128)(2,1)} %param.25, f32[640,1536]{1,0:T(8,128)S(1)} %fusion.22), kind=kOutput, calls=%fused_computation.41 | convolution fusion | flops 2836930560 | bytes 12042240 | tf_op jit(solution)/shard_map/dot_general | solution.py:165
  440.4 8.4 %reshape.327 = bf16[640,2880]{1,0:T(8,128)(2,1)} reshape(bf16[128,5,2880]{2,1,0:T(8,128)(2,1)} %all_to_all.10) | data formatting | bytes 7372800 | tf_op jit(solution)/shard_map/reshape | solution.py:163
  448.8 9.9 %fusion.24 = f32[640,1536]{1,0:T(8,128)S(1)} fusion(bf16[640,2880]{1,0:T(8,128)(2,1)} %reshape.327, bf16[1,2880,1536]{2,1,0:T(8,128)(2,1)} %param.24), kind=kOutput, calls=%fused_computation.37 | convolution fusion | flops 5662310400 | bytes 16465920 | tf_op jit(solution)/shard_map/dot_general | solution.py:163
  458.6 9.0 %add_convert_fusion = bf16[640,2880]{0,1:T(8,128)(2,1)} fusion(bf16[640,2880]{0,1:T(8,128)(2,1)} %collective-permute-done.3, bf16[1,768,2880]{1,2,0:T(8,128)(2,1)} %param.25, f32[640,1536]{1,0:T(8,128)S(1)} %fusion.24), kind=kOutput, calls=%fused_computation.39 | convolution fusion | flops 2844303360 | bytes 15728640 | tf_op jit(solution)/shard_map/dot_general | solution.py:165
  467.6 6.2 %copy.62 = bf16[640,2880]{1,0:T(8,128)(2,1)} copy(bf16[640,2880]{0,1:T(8,128)(2,1)} %add_convert_fusion) | data formatting | bytes 7372800 | tf_op jit(solution)/shard_map/convert_element_type | solution.py:170
  473.8 7.4 %reshape.329 = bf16[128,5,2880]{2,1,0:T(8,128)(2,1)} reshape(bf16[640,2880]{1,0:T(8,128)(2,1)} %copy.62) | data formatting | bytes 7372800 | tf_op jit(solution)/shard_map/reshape | solution.py:172
  481.1 5.2 all-to-all-start.1
  486.8 73.2 %all-to-all-done.1 = bf16[128,5,2880]{2,1,0:T(8,128)(2,1)} async-done(((bf16[128,5,2880]{2,1,0:T(8,128)(2,1)}), bf16[128,5,2880]{2,1,0:T(8,128)(2,1)}, u32[]{:S(2)}, u32[]{:S(2)}) %all-to-all-start.1) | async-done | bytes 3686432 | tf_op jit(solution)/shard_map/all_to_all | solution.py:171
  560.0 8.0 %reshape.330 = bf16[640,2880]{1,0:T(8,128)(2,1)} reshape(bf16[128,5,2880]{2,1,0:T(8,128)(2,1)} %all-to-all-done.1) | data formatting | bytes 7372800 | tf_op jit(solution)/shard_map/reshape | solution.py:178
  568.0 9.3 %gather_fusion = bf16[512,2880]{1,0:T(8,128)(2,1)} fusion(bf16[640,2880]{1,0:T(8,128)(2,1)} %reshape.330, s32[1024]{0:T(1024)S(1)} %pad_clamp_fusion), kind=kCustom, calls=%fused_computation.1 | custom fusion | bytes 5900288 | tf_op jit(solution)/shard_map/gather | solution.py:179
  577.3 6.5 %reshape.332 = f32[128,4,2880]{2,1,0:T(4,128)} reshape(bf16[512,2880]{1,0:T(8,128)(2,1)} %gather_fusion) | data formatting | bytes 8847360 | tf_op jit(solution)/shard_map/convert_element_type | solution.py:179
  583.8 7.0 %multiply_reduce_fusion = f32[128,2880]{1,0:T(8,128)S(1)} fusion(f32[128,4,2880]{2,1,0:T(4,128)} %reshape.332, f32[128,4]{1,0:T(8,128)S(1)} %copy.63), kind=kLoop, calls=%fused_computation.40 | loop fusion | flops 2580480 | bytes 7374848 | tf_op jit(solution)/shard_map/reduce_sum | solution.py:180
  592.5 2.4 fusion.51
  (118 shorter events, 24.1 us)
Async XLA Ops:
  7.2 3.6 copy-start
  7.2 4.9 copy-start.9
  7.2 5.3 copy-start.8
  7.2 5.4 copy-start.4
  7.2 105.5 %all-gather.3.cloned.1.call-start = ((), (), s32[]{:S(2)}) async-start(), calls=%async_computation.2 | async-start | bytes 13369344 | tf_op jit(solution)/shard_map/all_gather | solution.py:91
  10.7 260.0 %all-gather.5.cloned.1.call-start = ((), (), s32[]{:S(2)}) async-start(), calls=%async_computation.3 | async-start | bytes 6406144 | tf_op jit(solution)/shard_map/all_gather | solution.py:114
  269.2 2.7 collective-permute-start
  271.9 8.6 %copy-start.6 = (s32[1,128,4]{1,2,0:T(4,128)S(1)}, s32[1,128,4]{1,2,0:T(4,128)}, u32[]{:S(2)}) copy-start(s32[1,128,4]{1,2,0:T(4,128)} %param.23) | copy-start | bytes 6148
  277.2 1.6 copy-start.3
  278.7 6.8 %copy-start.7 = (f32[2880]{0:T(1024)S(1)}, f32[2880]{0:T(1024)}, u32[]{:S(2)}) copy-start(f32[2880]{0:T(1024)} %param.21) | copy-start | bytes 34564
  280.0 3.6 collective-permute-start.1
  285.6 306.9 %copy-start.2 = (bf16[128,2880]{0,1:T(8,128)(2,1)}, bf16[128,2880]{0,1:T(8,128)(2,1)S(1)}, u32[]{:S(2)}) copy-start(bf16[128,2880]{0,1:T(8,128)(2,1)S(1)} %get-tuple-element.287) | copy-start | bytes 2211844
  398.1 7.7 %collective-permute-start.2 = (bf16[128,5,2880]{0,2,1:T(8,128)(2,1)}, bf16[128,5,2880]{0,2,1:T(8,128)(2,1)}, u32[]{:S(2)}, u32[]{:S(2)}) collective-permute-start(bf16[128,5,2880]{0,2,1:T(8,128)(2,1)} %copy.60), channel_id=1, source_target_pairs={{0,1},{1,0},{2,3},{3,2},{4,5},{5,4},{6,7},{7,6},{8,9},{9,8},{10,11... | collective-permute-start | bytes 11059208 | tf_op jit(solution)/shard_map/ppermute | solution.py:160
  440.0 18.7 %collective-permute-start.3 = (bf16[640,2880]{0,1:T(8,128)(2,1)}, bf16[640,2880]{0,1:T(8,128)(2,1)}, u32[]{:S(2)}, u32[]{:S(2)}) collective-permute-start(bf16[640,2880]{0,1:T(8,128)(2,1)} %convolution_convert_fusion), channel_id=1, source_target_pairs={{0,1},{1,0},{2,3},{3,2},{4,5},{5,4},{6,7},{7,6},{8,9},{9,8},{10,11... | collective-permute-start | bytes 11059208 | tf_op jit(solution)/shard_map/ppermute | solution.py:169
  481.1 5.2 copy-start.5
  481.1 78.9 %all-to-all-start.1 = ((bf16[128,5,2880]{2,1,0:T(8,128)(2,1)}), bf16[128,5,2880]{2,1,0:T(8,128)(2,1)}, u32[]{:S(2)}, u32[]{:S(2)}) async-start(bf16[128,5,2880]{2,1,0:T(8,128)(2,1)} %reshape.329), calls=%async_computation.1 | async-start | bytes 12058624 | tf_op jit(solution)/shard_map/all_to_all | solution.py:171
  583.8 11.0 %copy-start.1 = (bf16[128,2880]{0,1:T(8,128)(2,1)S(1)}, bf16[128,2880]{0,1:T(8,128)(2,1)}, u32[]{:S(2)}) copy-start(bf16[128,2880]{0,1:T(8,128)(2,1)} %param.20) | copy-start | bytes 2211844
Sparse Core Ops, SparseCore 0:
  10.8 101.8 all-gather.2
  115.4 60.2 all-gather.4
where the time goes:
time: 612 us; the launch traced here: 602 us
  waiting for transfers between devices  181 us (30%)
  matrix products  130 us (21%)
  local copies, waits for them, and re-layouts  114 us (19%)
  blocking collectives  80.1 us (13%)
  other arithmetic  72.8 us (12%)
  between operations  14.5 us (2%)
  starting transfers between devices  8.92 us (1%)
    all_gather x1, waiting for transfers between devices, body(): piece = lax.all_gather(local_kv, 'ctx', axis=0, tiled=True)  99.8 us
    all_to_all x1, blocking collectives, body(): lax.all_to_all(split, ('ctx', 'grp'), split_axis=0, concat_axis=0, tiled=...  80.1 us
    all_to_all x1, waiting for transfers between devices, body(): lax.all_to_all(summed.reshape(owners, half_cap, width), ('ctx', 'grp'), s...  73.2 us
    reduce_sum x6, other arithmetic, key_block(): total = total * shrink + jnp.sum(weights, axis=-1)  54.9 us
    dot_general x6, matrix products, key_block(): jnp.einsum('kgqs,skd->kgqd', weights.astype(jnp.bfloat16), values, prefer...  44.9 us
    dot_general x6, matrix products, key_block(): jnp.einsum('qkgd,skd->kgqs', query_heads, keys, preferred_element_type=jn...  42.6 us
    dot_general x2, matrix products, expert_half(): jnp.dot(rows.reshape(-1, width), in_weights, preferred_element_type=jnp.f...  19.7 us
    dot_general x2, matrix products, expert_half(): jnp.dot(hidden, out_weights, preferred_element_type=jnp.float32)  16.8 us
  transfers between devices with their start and end apart: 7, of which 5 were waited for; matrix products, arithmetic and copies ran while one was open for 30% of the time, Pallas kernels for 0%

commit v1 on v0

--- a/solution.py
+++ b/solution.py
@@ -88,7 +88,9 @@
     start_top = jnp.broadcast_to(sink_grid[:, :, None], (KVH, groups, tokens))
     start_total = jnp.zeros((KVH, groups, tokens), jnp.float32)
     start_numer = jnp.zeros((KVH, groups, tokens, HD), jnp.float32)
-    piece = lax.all_gather(local_kv, "ctx", axis=0, tiled=True)
+    piece = jnp.concatenate(
+        lax.all_to_all(jnp.stack([local_kv] * lax.axis_size("ctx")), "ctx", 0, 0), axis=0
+    )
     count = piece.shape[0]
     step_rows = math.gcd(count, 1024)
 

time: 612 us -> 779 us (1.27)
  waiting for transfers between devices: 181 us -> 295 us
  local copies, waits for them, and re-layouts: 114 us -> 152 us
  starting transfers between devices: 8.92 us -> 17 us
    all_to_all x0 -> x1, waiting for transfers between devices: none -> 214 us  [body(): lax.all_to_all(jnp.stack([local_kv] * lax.axis_size('ctx')), 'ctx', 0, 0)]
    all_gather x1 -> x0, waiting for transfers between devices: 99.8 us -> none  [body(): piece = lax.all_gather(local_kv, 'ctx', axis=0, tiled=True)]
    all_to_all x0 -> x1, local copies, waits for them, and re-layouts: none -> 16.6 us  [body(): lax.all_to_all(jnp.stack([local_kv] * lax.axis_size('ctx')), 'ctx', 0, 0)]
    while x6 -> x18, local copies, waits for them, and re-layouts: 0.02 us -> 12.1 us
  transfers between devices with their start and end apart: 7 -> 7, of which waited for: 5 -> 5; matrix products, arithmetic and copies ran while one was open for 30% -> 29% of each run, Pallas kernels for 0% -> 0%
where the time goes in v1:
time: 779 us; the launch traced here: 768 us
  waiting for transfers between devices  295 us (38%)
  local copies, waits for them, and re-layouts  152 us (20%)
  matrix products  136 us (17%)
  blocking collectives  78.7 us (10%)
  other arithmetic  73.9 us (9%)
  starting transfers between devices  17 us (2%)
  between operations  14.5 us (2%)
    all_to_all x1, waiting for transfers between devices, body(): lax.all_to_all(jnp.stack([local_kv] * lax.axis_size('ctx')), 'ctx', 0, 0)  214 us
    all_to_all x1, blocking collectives, body(): lax.all_to_all(split, ('ctx', 'grp'), split_axis=0, concat_axis=0, tiled=...  78.7 us
    all_to_all x1, waiting for transfers between devices, body(): lax.all_to_all(summed.reshape(owners, half_cap, width), ('ctx', 'grp'), s...  73.2 us
    reduce_sum x6, other arithmetic, key_block(): total = total * shrink + jnp.sum(weights, axis=-1)  54.5 us
    dot_general x6, matrix products, key_block(): jnp.einsum('kgqs,skd->kgqd', weights.astype(jnp.bfloat16), values, prefer...  51.9 us
    dot_general x6, matrix products, key_block(): jnp.einsum('qkgd,skd->kgqs', query_heads, keys, preferred_element_type=jn...  42.3 us
    dot_general x2, matrix products, expert_half(): jnp.dot(rows.reshape(-1, width), in_weights, preferred_element_type=jnp.f...  19.7 us
    dot_general x2, matrix products, expert_half(): jnp.dot(hidden, out_weights, preferred_element_type=jnp.float32)  16.8 us
  transfers between devices with their start and end apart: 7, of which 5 were waited for; matrix products, arithmetic and copies ran while one was open for 29% of the time, Pallas kernels for 0%

profile of v1, /device:TPU:1, one launch (start us, length us, event | category | flops | bytes accessed | tf_op | source)
XLA Modules:
  0.0 768.4 jit_solution(3767584308005152845)
XLA Ops:
  8.8 6.1 stack.2
  14.9 7.8 %all-to-all-start = ((bf16[16,384,1024]{1,2,0:T(8,128)(2,1)}), bf16[16,384,1024]{1,2,0:T(8,128)(2,1)}, u32[]{:S(2)}, u32[]{:S(2)}) async-start(bf16[16,384,1024]{1,2,0:T(8,128)(2,1)} %stack.2), calls=%async_computation | async-start | bytes 25165824 | tf_op jit(solution)/shard_map/all_to_all | solution.py:92
  24.9 213.6 %all-to-all-done = bf16[16,384,1024]{1,2,0:T(8,128)(2,1)} async-done(((bf16[16,384,1024]{1,2,0:T(8,128)(2,1)}), bf16[16,384,1024]{1,2,0:T(8,128)(2,1)}, u32[]{:S(2)}, u32[]{:S(2)}) %all-to-all-start) | async-done | bytes 12582944 | tf_op jit(solution)/shard_map/all_to_all | solution.py:92
  238.5 16.6 %copy.66 = bf16[16,384,1024]{2,1,0:T(8,128)(2,1)} copy(bf16[16,384,1024]{1,2,0:T(8,128)(2,1)} %all-to-all-done) | data formatting | bytes 25165824 | tf_op jit(solution)/shard_map/all_to_all | solution.py:92
  255.2 180.0 %while.20 = (s32[]{:T(128)}, f32[8,4,128]{2,1,0:T(4,128)S(1)}, f32[8,4,128]{2,1,0:T(4,128)S(1)}, f32[8,4,128,64]{2,3,1,0:T(8,128)}, s32[1,8]{1,0:T(1,128)S(1)}, ...) while((s32[]{:T(128)}, f32[8,4,128]{2,1,0:T(4,128)S(1)}, ...), condition=%wide.region_7.8_spmd.clone, body=%wide.region_3.7_spmd.clone.sunk | while | flops 1121116288 | bytes 64247544 | solution.py:102
  255.2 2.7 fusion.88
  259.8 7.0 fusion.89
  266.9 9.1 %fusion.90 = f32[8,4,128]{2,1,0:T(4,128)S(1)} fusion(f32[8,1024,128,4]{2,1,3,0:T(8,128)} %get-tuple-element.375, f32[8,4,128]{2,1,0:T(4,128)S(1)} %max.12, pred[128,1024]{0,1:T(8,128)(4,1)S(1)} %compare_and_fusion.2), kind=kLoop, calls=%fused_computation.10.clone.1 | loop fusion | flops 16773120 | bytes 16941056 | tf_op jit(solution)/shard_map/while/body/eval_jaxpr/reduce_sum | solution.py:79
  276.5 8.4 %fusion.92 = f32[8,4,128,64]{2,3,1,0:T(8,128)} fusion(bf16[1024,8,64,1]{0,2,3,1:T(8,128)(2,1)S(1)} %bitcast.105, f32[8,1024,128,4]{2,1,3,0:T(8,128)} %get-tuple-element.375, f32[8,4,128]{2,1,0:T(4,128)S(1)} %max.12, pred[128,1024]{0,1:T(8,128)(4,1)S(1)} %compare_and_fusion.2, f32[8,4,128,64]{2,3,1,0:T(8,128)} %get-tuple-element.396, ...), kind=kOutput, calls=%fused_computation.13.clone.1 | convolution fusion | flops 554434560 | bytes 20086784 | tf_op jit(solution)/shard_map/while/body/eval_jaxpr/kgqs,skd->kgqd/dot_general | solution.py:80
  285.0 2.7 fusion.88
  289.6 7.0 fusion.89
  296.6 9.1 %fusion.90 = f32[8,4,128]{2,1,0:T(4,128)S(1)} fusion(f32[8,1024,128,4]{2,1,3,0:T(8,128)} %get-tuple-element.375, f32[8,4,128]{2,1,0:T(4,128)S(1)} %max.12, pred[128,1024]{0,1:T(8,128)(4,1)S(1)} %compare_and_fusion.2), kind=kLoop, calls=%fused_computation.10.clone.1 | loop fusion | flops 16773120 | bytes 16941056 | tf_op jit(solution)/shard_map/while/body/eval_jaxpr/reduce_sum | solution.py:79
  306.3 8.7 %fusion.92 = f32[8,4,128,64]{2,3,1,0:T(8,128)} fusion(bf16[1024,8,64,1]{0,2,3,1:T(8,128)(2,1)S(1)} %bitcast.105, f32[8,1024,128,4]{2,1,3,0:T(8,128)} %get-tuple-element.375, f32[8,4,128]{2,1,0:T(4,128)S(1)} %max.12, pred[128,1024]{0,1:T(8,128)(4,1)S(1)} %compare_and_fusion.2, f32[8,4,128,64]{2,3,1,0:T(8,128)} %get-tuple-element.396, ...), kind=kOutput, calls=%fused_computation.13.clone.1 | convolution fusion | flops 554434560 | bytes 20086784 | tf_op jit(solution)/shard_map/while/body/eval_jaxpr/kgqs,skd->kgqd/dot_general | solution.py:80
  315.0 2.7 fusion.88
  319.6 7.0 fusion.89
  326.7 9.1 %fusion.90 = f32[8,4,128]{2,1,0:T(4,128)S(1)} fusion(f32[8,1024,128,4]{2,1,3,0:T(8,128)} %get-tuple-element.375, f32[8,4,128]{2,1,0:T(4,128)S(1)} %max.12, pred[128,1024]{0,1:T(8,128)(4,1)S(1)} %compare_and_fusion.2), kind=kLoop, calls=%fused_computation.10.clone.1 | loop fusion | flops 16773120 | bytes 16941056 | tf_op jit(solution)/shard_map/while/body/eval_jaxpr/reduce_sum | solution.py:79
  336.3 8.7 %fusion.92 = f32[8,4,128,64]{2,3,1,0:T(8,128)} fusion(bf16[1024,8,64,1]{0,2,3,1:T(8,128)(2,1)S(1)} %bitcast.105, f32[8,1024,128,4]{2,1,3,0:T(8,128)} %get-tuple-element.375, f32[8,4,128]{2,1,0:T(4,128)S(1)} %max.12, pred[128,1024]{0,1:T(8,128)(4,1)S(1)} %compare_and_fusion.2, f32[8,4,128,64]{2,3,1,0:T(8,128)} %get-tuple-element.396, ...), kind=kOutput, calls=%fused_computation.13.clone.1 | convolution fusion | flops 554434560 | bytes 20086784 | tf_op jit(solution)/shard_map/while/body/eval_jaxpr/kgqs,skd->kgqd/dot_general | solution.py:80
  345.0 2.7 fusion.88
  349.7 7.0 fusion.89
  356.7 9.1 %fusion.90 = f32[8,4,128]{2,1,0:T(4,128)S(1)} fusion(f32[8,1024,128,4]{2,1,3,0:T(8,128)} %get-tuple-element.375, f32[8,4,128]{2,1,0:T(4,128)S(1)} %max.12, pred[128,1024]{0,1:T(8,128)(4,1)S(1)} %compare_and_fusion.2), kind=kLoop, calls=%fused_computation.10.clone.1 | loop fusion | flops 16773120 | bytes 16941056 | tf_op jit(solution)/shard_map/while/body/eval_jaxpr/reduce_sum | solution.py:79
  366.4 8.7 %fusion.92 = f32[8,4,128,64]{2,3,1,0:T(8,128)} fusion(bf16[1024,8,64,1]{0,2,3,1:T(8,128)(2,1)S(1)} %bitcast.105, f32[8,1024,128,4]{2,1,3,0:T(8,128)} %get-tuple-element.375, f32[8,4,128]{2,1,0:T(4,128)S(1)} %max.12, pred[128,1024]{0,1:T(8,128)(4,1)S(1)} %compare_and_fusion.2, f32[8,4,128,64]{2,3,1,0:T(8,128)} %get-tuple-element.396, ...), kind=kOutput, calls=%fused_computation.13.clone.1 | convolution fusion | flops 554434560 | bytes 20086784 | tf_op jit(solution)/shard_map/while/body/eval_jaxpr/kgqs,skd->kgqd/dot_general | solution.py:80
  379.7 7.0 fusion.89
  386.8 9.1 %fusion.90 = f32[8,4,128]{2,1,0:T(4,128)S(1)} fusion(f32[8,1024,128,4]{2,1,3,0:T(8,128)} %get-tuple-element.375, f32[8,4,128]{2,1,0:T(4,128)S(1)} %max.12, pred[128,1024]{0,1:T(8,128)(4,1)S(1)} %compare_and_fusion.2), kind=kLoop, calls=%fused_computation.10.clone.1 | loop fusion | flops 16773120 | bytes 16941056 | tf_op jit(solution)/shard_map/while/body/eval_jaxpr/reduce_sum | solution.py:79
  396.4 8.7 %fusion.92 = f32[8,4,128,64]{2,3,1,0:T(8,128)} fusion(bf16[1024,8,64,1]{0,2,3,1:T(8,128)(2,1)S(1)} %bitcast.105, f32[8,1024,128,4]{2,1,3,0:T(8,128)} %get-tuple-element.375, f32[8,4,128]{2,1,0:T(4,128)S(1)} %max.12, pred[128,1024]{0,1:T(8,128)(4,1)S(1)} %compare_and_fusion.2, f32[8,4,128,64]{2,3,1,0:T(8,128)} %get-tuple-element.396, ...), kind=kOutput, calls=%fused_computation.13.clone.1 | convolution fusion | flops 554434560 | bytes 20086784 | tf_op jit(solution)/shard_map/while/body/eval_jaxpr/kgqs,skd->kgqd/dot_general | solution.py:80
  409.8 7.0 fusion.89
  416.8 9.1 %fusion.90 = f32[8,4,128]{2,1,0:T(4,128)S(1)} fusion(f32[8,1024,128,4]{2,1,3,0:T(8,128)} %get-tuple-element.375, f32[8,4,128]{2,1,0:T(4,128)S(1)} %max.12, pred[128,1024]{0,1:T(8,128)(4,1)S(1)} %compare_and_fusion.2), kind=kLoop, calls=%fused_computation.10.clone.1 | loop fusion | flops 16773120 | bytes 16941056 | tf_op jit(solution)/shard_map/while/body/eval_jaxpr/reduce_sum | solution.py:79
  426.5 8.7 %fusion.92 = f32[8,4,128,64]{2,3,1,0:T(8,128)} fusion(bf16[1024,8,64,1]{0,2,3,1:T(8,128)(2,1)S(1)} %bitcast.105, f32[8,1024,128,4]{2,1,3,0:T(8,128)} %get-tuple-element.375, f32[8,4,128]{2,1,0:T(4,128)S(1)} %max.12, pred[128,1024]{0,1:T(8,128)(4,1)S(1)} %compare_and_fusion.2, f32[8,4,128,64]{2,3,1,0:T(8,128)} %get-tuple-element.396, ...), kind=kOutput, calls=%fused_computation.13.clone.1 | convolution fusion | flops 554434560 | bytes 20086784 | tf_op jit(solution)/shard_map/while/body/eval_jaxpr/kgqs,skd->kgqd/dot_general | solution.py:80
  439.9 5.3 fusion.52
  454.3 16.3 %scatter_custom_fusion = bf16[640,2880]{1,0:T(8,128)(2,1)} fusion(s32[512]{0:T(512)S(1)} %bitcast.115, bf16[128,2880]{1,0:T(8,128)(2,1)S(1)} %copy.74, s32[1024]{0:T(1024)S(1)} %pad_clamp_fusion.1, bf16[]{:T(256)} %constant.192.clone.1), kind=kCustom, calls=%fused_computation.45 | custom fusion | bytes 3686402 | tf_op jit(solution)/shard_map/scatter | solution.py:153
  470.6 7.4 reshape_reshape.3
  478.0 78.7 %all_to_all.15 = bf16[128,5,2880]{2,1,0:T(8,128)(2,1)} all-to-all(bf16[128,5,2880]{2,1,0:T(8,128)(2,1)} %reshape_reshape.3), channel_id=1, replica_groups=mesh['ctx'=16,'grp'=8] {'ctx','grp'}, dimensions={0} | all-to-all | bytes 7372800 | tf_op jit(solution)/shard_map/all_to_all | solution.py:161
  556.7 7.9 %copy.75 = bf16[128,5,2880]{0,2,1:T(8,128)(2,1)} copy(bf16[128,5,2880]{2,1,0:T(8,128)(2,1)} %all_to_all.15) | data formatting | bytes 7372800 | tf_op jit(solution)/shard_map/all_to_all | solution.py:161
  565.9 6.4 collective-permute-done.2
  572.3 8.5 %copy.76 = bf16[128,5,2880]{2,1,0:T(8,128)(2,1)} copy(bf16[128,5,2880]{0,2,1:T(8,128)(2,1)} %collective-permute-done.2) | data formatting | bytes 7372800 | tf_op jit(solution)/shard_map/ppermute | solution.py:162
  580.8 8.0 %reshape.334 = bf16[640,2880]{1,0:T(8,128)(2,1)} reshape(bf16[128,5,2880]{2,1,0:T(8,128)(2,1)} %copy.76) | data formatting | bytes 7372800 | tf_op jit(solution)/shard_map/reshape | solution.py:165
  588.8 9.9 %fusion.22 = f32[640,1536]{1,0:T(8,128)S(1)} fusion(bf16[640,2880]{1,0:T(8,128)(2,1)} %reshape.334, bf16[1,2880,1536]{2,1,0:T(8,128)(2,1)} %param.24), kind=kOutput, calls=%fused_computation.35 | convolution fusion | flops 5662310400 | bytes 16465920 | tf_op jit(solution)/shard_map/dot_general | solution.py:165
  598.7 7.9 %convolution_convert_fusion = bf16[640,2880]{0,1:T(8,128)(2,1)} fusion(bf16[1,768,2880]{1,2,0:T(8,128)(2,1)} %param.25, f32[640,1536]{1,0:T(8,128)S(1)} %fusion.22), kind=kOutput, calls=%fused_computation.41 | convolution fusion | flops 2836930560 | bytes 12042240 | tf_op jit(solution)/shard_map/dot_general | solution.py:167
  606.9 8.4 %reshape.333 = bf16[640,2880]{1,0:T(8,128)(2,1)} reshape(bf16[128,5,2880]{2,1,0:T(8,128)(2,1)} %all_to_all.15) | data formatting | bytes 7372800 | tf_op jit(solution)/shard_map/reshape | solution.py:165
  615.3 9.9 %fusion.24 = f32[640,1536]{1,0:T(8,128)S(1)} fusion(bf16[640,2880]{1,0:T(8,128)(2,1)} %reshape.333, bf16[1,2880,1536]{2,1,0:T(8,128)(2,1)} %param.24), kind=kOutput, calls=%fused_computation.37 | convolution fusion | flops 5662310400 | bytes 16465920 | tf_op jit(solution)/shard_map/dot_general | solution.py:165
  625.2 9.0 %add_convert_fusion = bf16[640,2880]{0,1:T(8,128)(2,1)} fusion(bf16[640,2880]{0,1:T(8,128)(2,1)} %collective-permute-done.3, bf16[1,768,2880]{1,2,0:T(8,128)(2,1)} %param.25, f32[640,1536]{1,0:T(8,128)S(1)} %fusion.24), kind=kOutput, calls=%fused_computation.39 | convolution fusion | flops 2844303360 | bytes 15728640 | tf_op jit(solution)/shard_map/dot_general | solution.py:167
  634.1 6.2 copy.77
  640.3 7.4 reshape.335
  647.7 5.2 all-to-all-start.2
  653.3 73.2 %all-to-all-done.2 = bf16[128,5,2880]{2,1,0:T(8,128)(2,1)} async-done(((bf16[128,5,2880]{2,1,0:T(8,128)(2,1)}), bf16[128,5,2880]{2,1,0:T(8,128)(2,1)}, u32[]{:S(2)}, u32[]{:S(2)}) %all-to-all-start.2) | async-done | bytes 3686432 | tf_op jit(solution)/shard_map/all_to_all | solution.py:173
  726.5 8.0 %reshape.336 = bf16[640,2880]{1,0:T(8,128)(2,1)} reshape(bf16[128,5,2880]{2,1,0:T(8,128)(2,1)} %all-to-all-done.2) | data formatting | bytes 7372800 | tf_op jit(solution)/shard_map/reshape | solution.py:180
  734.5 9.3 %gather_fusion = bf16[512,2880]{1,0:T(8,128)(2,1)} fusion(bf16[640,2880]{1,0:T(8,128)(2,1)} %reshape.336, s32[1024]{0:T(1024)S(1)} %pad_clamp_fusion), kind=kCustom, calls=%fused_computation.1 | custom fusion | bytes 5900288 | tf_op jit(solution)/shard_map/gather | solution.py:181
  743.8 6.5 reshape.338
  750.4 7.0 multiply_reduce_fusion
  (130 shorter events, 43.9 us)
Async XLA Ops:
  7.2 15.6 %copy-start = (bf16[128,2880]{0,1:T(8,128)(2,1)S(1)}, bf16[128,2880]{0,1:T(8,128)(2,1)}, u32[]{:S(2)}) copy-start(bf16[128,2880]{0,1:T(8,128)(2,1)} %param.20) | copy-start | bytes 2211844
  14.9 9.2 %copy-start.9 = (s32[1,8]{1,0:T(1,128)S(1)}, s32[1,8]{1,0:T(1,128)}, u32[]{:S(2)}) copy-start(s32[1,8]{1,0:T(1,128)} %param.18) | copy-start | bytes 100
  14.9 9.6 %copy-start.8 = (f32[32]{0:T(128)S(1)}, f32[32]{0:T(128)}, u32[]{:S(2)}) copy-start(f32[32]{0:T(128)} %param.19) | copy-start | bytes 388
  14.9 9.6 %copy-start.4 = (bf16[1,128,2048]{2,1,0:T(8,128)(2,1)S(1)}, bf16[1,128,2048]{2,1,0:T(8,128)(2,1)}, u32[]{:S(2)}) copy-start(bf16[1,128,2048]{2,1,0:T(8,128)(2,1)} %param.15) | copy-start | bytes 1572868
  14.9 223.6 %all-to-all-start = ((bf16[16,384,1024]{1,2,0:T(8,128)(2,1)}), bf16[16,384,1024]{1,2,0:T(8,128)(2,1)}, u32[]{:S(2)}, u32[]{:S(2)}) async-start(bf16[16,384,1024]{1,2,0:T(8,128)(2,1)} %stack.2), calls=%async_computation | async-start | bytes 25165824 | tf_op jit(solution)/shard_map/all_to_all | solution.py:92
  22.7 416.1 %all-gather.2.cloned.1.call-start = ((), (), s32[]{:S(2)}) async-start(), calls=%async_computation.3 | async-start | bytes 6406144 | tf_op jit(solution)/shard_map/all_gather | solution.py:116
  436.7 3.2 collective-permute-start
  439.9 8.5 %copy-start.6 = (s32[1,128,4]{1,2,0:T(4,128)S(1)}, s32[1,128,4]{1,2,0:T(4,128)}, u32[]{:S(2)}) copy-start(s32[1,128,4]{1,2,0:T(4,128)} %param.23) | copy-start | bytes 6148
  445.2 1.6 copy-start.3
  446.8 6.7 copy-start.7
  448.0 3.5 collective-permute-start.1
  453.5 305.5 %copy-start.2 = (bf16[128,2880]{0,1:T(8,128)(2,1)}, bf16[128,2880]{0,1:T(8,128)(2,1)S(1)}, u32[]{:S(2)}) copy-start(bf16[128,2880]{0,1:T(8,128)(2,1)S(1)} %get-tuple-element.305) | copy-start | bytes 2211844
  564.6 7.7 collective-permute-start.2
  606.5 18.6 %collective-permute-start.3 = (bf16[640,2880]{0,1:T(8,128)(2,1)}, bf16[640,2880]{0,1:T(8,128)(2,1)}, u32[]{:S(2)}, u32[]{:S(2)}) collective-permute-start(bf16[640,2880]{0,1:T(8,128)(2,1)} %convolution_convert_fusion), channel_id=1, source_target_pairs={{0,1},{1,0},{2,3},{3,2},{4,5},{5,4},{6,7},{7,6},{8,9},{9,8},{10,11... | collective-permute-start | bytes 11059208 | tf_op jit(solution)/shard_map/ppermute | solution.py:171
  647.7 5.2 copy-start.5
  647.7 78.9 %all-to-all-start.2 = ((bf16[128,5,2880]{2,1,0:T(8,128)(2,1)}), bf16[128,5,2880]{2,1,0:T(8,128)(2,1)}, u32[]{:S(2)}, u32[]{:S(2)}) async-start(bf16[128,5,2880]{2,1,0:T(8,128)(2,1)} %reshape.335), calls=%async_computation.2 | async-start | bytes 12058624 | tf_op jit(solution)/shard_map/all_to_all | solution.py:173
  750.4 11.0 %copy-start.1 = (bf16[128,2880]{0,1:T(8,128)(2,1)S(1)}, bf16[128,2880]{0,1:T(8,128)(2,1)}, u32[]{:S(2)}) copy-start(bf16[128,2880]{0,1:T(8,128)(2,1)} %param.20) | copy-start | bytes 2211844
Sparse Core Ops, SparseCore 0:
  26.2 207.7 all-gather.1
